TPU v7x, 32 devices: a whole 2x2x4 slice. The times are simulated.
32 devices in a mesh: ep: 8 (over z, x), tp: 4 (over y, core).
Axes of the slice: x: 2, y: 2, z: 4, core: 2. Of those that a mesh axis runs over, the one named last changes fastest.
Arguments:
- features: bfloat16 [2048, 1024], P('ep'), may hold values from -6 to 6
- cotangent: bfloat16 [2048, 2048], P('ep'), may hold values from -6 to 6
- expert_ids: int32 [2048, 2], P('ep'), may hold values from 0 to 7, all different within a row; in each aligned block of 256 rows (0 to 255, 256 to 511, ...) at most 96 rows name the same one
- gate_levels: int32 [2048, 2], P('ep'), may hold values from 1 to 15
- w_in: bfloat16 [8, 1024, 4096], P('ep', None, 'tp'), may hold values from -0.1875 to 0.1875
- w_out: bfloat16 [8, 4096, 2048], P('ep', 'tp'), may hold values from -0.09375 to 0.09375
Outputs:
- grad_in: bfloat16 [2048, 1024], P('ep', 'tp')
- grad_w_in: bfloat16 [8, 1024, 4096], P('ep', None, 'tp')
- grad_w_out: bfloat16 [8, 4096, 2048], P('ep', 'tp')
Inputs may be any that keep to these rules, and one draw needn't show every extreme that they name: `expert_ids`: each row names two different experts. In each aligned block of 256 rows no expert is named by more than 96 rows, and some expert reaches 96 rows in some block.
All inputs are finite; a program needn't handle non-finite values.
Results may differ from a plain program's by a relative error of at most 0.0065.
Values may be sent and summed in bfloat16 or wider, within the bound.
No kernel may reach another device: no remote copies, remote signals or barrier semaphores. Data moves between devices by JAX's collectives and lax.ppermute only.
A program may use at most 128 MiB of HBM per device.

v0:
```python
import math
import jax
import jax.numpy as jnp
from jax import lax
from jax.sharding import PartitionSpec as P

E = 8


def shifted(value, axis, by):
    peers = lax.axis_size(axis)
    return lax.ppermute(value, axis, [(i, (i + by) % peers) for i in range(peers)])


def slot_positions(expert_ids, blocks, experts, capacity):
    flattened = expert_ids.reshape(blocks, -1)
    one_hot = (flattened[:, :, None] == jnp.arange(experts, dtype=jnp.int32)[None, None, :]).astype(
        jnp.int32
    )
    earlier = jnp.cumsum(one_hot, axis=1) - one_hot
    within = jnp.sum(one_hot * earlier, axis=2)
    block_ids = jnp.arange(blocks, dtype=jnp.int32)[:, None]
    return ((block_ids * experts + flattened) * capacity + within).reshape(-1)


def chip_then_link_sum(partial, j):
    quarter = partial.shape[0] // 4

    def rows(q):
        return lax.dynamic_slice_in_dim(partial, q * quarter, quarter, 0)

    keep = jnp.concatenate([rows(j), rows(j ^ 2)], axis=0)
    give = jnp.concatenate([rows(j ^ 1), rows(j ^ 3)], axis=0)
    keep = keep + lax.ppermute(give, "tp", [(i, i ^ 1) for i in range(4)])
    mine, send = (keep[:quarter], keep[quarter:])
    moved = lax.ppermute(send.astype(jnp.bfloat16), "tp", [(i, i ^ 2) for i in range(4)])
    return mine + moved.astype(jnp.float32)


def shards(features, cotangent, expert_ids, gate_levels, w_in, w_out):
    device_count = lax.axis_size("ep")
    replicas = device_count // E
    replica = lax.axis_index("ep") // E
    tokens_here = expert_ids.shape[0]
    sub_rows = tokens_here // replicas
    capacity = 3 * sub_rows // 8
    slot_count = device_count * capacity
    pair_count = 2 * tokens_here
    positions = slot_positions(expert_ids, replicas, E, capacity)
    slot_ids = jnp.arange(slot_count, dtype=jnp.int32)[:, None]
    choices = positions.reshape(tokens_here, 2)
    first_hit = choices[None, :, 0] == slot_ids
    second_hit = choices[None, :, 1] == slot_ids
    gates = gate_levels.astype(jnp.float32) / 16.0
    pick = (first_hit | second_hit).astype(jnp.bfloat16)
    pick_scaled = jnp.where(
        first_hit, gates[None, :, 0], jnp.where(second_hit, gates[None, :, 1], 0.0)
    ).astype(jnp.bfloat16)
    tp_size = lax.axis_size("tp")
    tp_index = lax.axis_index("tp")
    split = 4 if tp_size == 4 else 2 if tp_size % 2 == 0 else 1

    def dispatched(table, selection):
        width = table.shape[1] // split
        part = tp_index % split
        mine = lax.dynamic_slice_in_dim(table, part * width, width, 1)
        mine = jnp.dot(selection, mine, preferred_element_type=jnp.float32).astype(jnp.bfloat16)
        mine = lax.all_to_all(mine, "ep", split_axis=0, concat_axis=0, tiled=True)
        pieces = [(mine, part)]
        if split == 4:
            across = lax.ppermute(mine, "tp", [(i, i ^ 2) for i in range(tp_size)])
            pieces.append((across, part ^ 2))
        if split >= 2:
            pieces += [
                (lax.ppermute(piece, "tp", [(i, i ^ 1) for i in range(tp_size)]), where ^ 1)
                for piece, where in pieces
            ]
        if split == 1:
            return mine
        whole = jnp.zeros((mine.shape[0], table.shape[1]), jnp.bfloat16)
        for piece, where in pieces:
            whole = lax.dynamic_update_slice_in_dim(whole, piece, where * width, 1)
        return whole

    rows_x = dispatched(features, pick)
    rows_dy = dispatched(cotangent, pick_scaled)
    piece_in = w_in[0]
    piece_out = w_out[0]
    span = piece_in.shape[1]
    weight_in = jnp.zeros((piece_in.shape[0], span * replicas), jnp.bfloat16)
    weight_out = jnp.zeros((span * replicas, piece_out.shape[1]), jnp.bfloat16)
    weight_in = lax.dynamic_update_slice_in_dim(weight_in, piece_in, replica * span, 1)
    weight_out = lax.dynamic_update_slice_in_dim(weight_out, piece_out, replica * span, 0)
    moving = (piece_in, piece_out)
    for turn_index in range(1, replicas):
        moving = shifted((moving[0], moving[1]), "ep", E)
        anchor = (replica - turn_index) % replicas
        weight_in = lax.dynamic_update_slice_in_dim(weight_in, moving[0], anchor * span, 1)
        weight_out = lax.dynamic_update_slice_in_dim(weight_out, moving[1], anchor * span, 0)
    pre = jnp.dot(rows_x, weight_in, preferred_element_type=jnp.float32)
    activated, gelu_back = jax.vjp(jax.nn.gelu, pre)
    act_rows = lax.optimization_barrier(activated.astype(jnp.bfloat16))
    back_act = lax.dot_general(
        rows_dy, weight_out, (((1,), (1,)), ((), ())), preferred_element_type=jnp.float32
    )
    back_pre = gelu_back(back_act)[0].astype(jnp.bfloat16)
    partial = lax.dot_general(
        weight_in, back_pre, (((1,), (1,)), ((), ())), preferred_element_type=jnp.float32
    )
    if tp_size == 4:
        summed = chip_then_link_sum(partial, tp_index)
    else:
        summed = lax.psum_scatter(partial, "tp", scatter_dimension=0, tiled=True)
    returned = lax.all_to_all(
        summed.astype(jnp.bfloat16), "ep", split_axis=1, concat_axis=1, tiled=True
    )
    grad_in = lax.dot_general(
        pick, returned, (((0,), (1,)), ((), ())), preferred_element_type=jnp.float32
    ).astype(jnp.bfloat16)

    def span_grads(first_span, span_total):
        width = span_total * span
        act_cols = lax.dynamic_slice_in_dim(act_rows, first_span * span, width, 1)
        pre_cols = lax.dynamic_slice_in_dim(back_pre, first_span * span, width, 1)
        grad_first = lax.dot_general(
            pre_cols, rows_x, (((0,), (0,)), ((), ())), preferred_element_type=jnp.float32
        )
        grad_second = lax.dot_general(
            act_cols, rows_dy, (((0,), (0,)), ((), ())), preferred_element_type=jnp.float32
        )
        return (grad_first, grad_second)

    summed_grads = span_grads((replica - 1) % replicas, 1)
    for turn_index in range(1, replicas):
        summed_grads = shifted((summed_grads[0], summed_grads[1]), "ep", E)
        own_grads = span_grads((replica - turn_index - 1) % replicas, 1)
        summed_grads = (summed_grads[0] + own_grads[0], summed_grads[1] + own_grads[1])
    grad_scale = 1.0 / math.sqrt(2.0 * tokens_here * device_count / E)
    grad_w_in = (summed_grads[0] * grad_scale).T.astype(jnp.bfloat16)[None]
    grad_w_out = (summed_grads[1] * grad_scale).astype(jnp.bfloat16)[None]
    return (grad_in, grad_w_in, grad_w_out)


def solution(mesh):
    return jax.shard_map(
        shards,
        mesh=mesh,
        in_specs=(
            P("ep", None),
            P("ep", None),
            P("ep", None),
            P("ep", None),
            P("ep", None, "tp"),
            P("ep", "tp", None),
        ),
        out_specs=(P("ep", "tp"), P("ep", None, "tp"), P("ep", "tp", None)),
        check_vma=False,
    )
```

profile of v0, /device:TPU:0, one launch (start us, length us, event | category | flops | bytes accessed | tf_op | source)
XLA Modules:
  0.0 114.2 jit_solution(2538549996480562133)
XLA Ops:
  0.7 1.0 copy.15
  1.8 1.1 %reduce-window.6 = s32[1,8,4,128]{3,1,2,0:T(8,128)S(1)} reduce-window(s32[1,8,4,128]{3,1,2,0:T(8,128)S(1)} %convert_bitcast_fusion, s32[]{:T(128)} %constant.31.clone.1), window={size=1x1x1x128 pad=0_0x0_0x0_0x127_0}, to_apply=%region_0.1 | reduce-window | flops 520192 | bytes 32772 | tf_op jit(solution)/shard_map/reduce-window
  3.5 0.7 multiply_add_fusion
  4.2 1.9 %convolution_convert_fusion.1 = bf16[768,256]{1,0:T(8,128)(2,1)} fusion(s32[256]{0:T(256)S(1)} %bitcast.69, s32[256]{0:T(256)S(1)} %bitcast.66, bf16[256,1024]{1,0:T(8,128)(2,1)} %param.6, s32[]{:T(128)S(6)} %select_n.70), kind=kOutput, calls=%fused_computation.23 | convolution fusion | flops 101449728 | bytes 526340 | tf_op jit(solution)/shard_map/dot_general | solution.py:67
  6.2 7.3 %all-to-all-start.1 = ((bf16[8,96,256]{2,1,0:T(8,128)(2,1)}), bf16[8,96,256]{2,1,0:T(8,128)(2,1)S(1)}, u32[]{:S(2)}, u32[]{:S(2)}) async-start(bf16[8,96,256]{2,1,0:T(8,128)(2,1)} %bitcast.13), calls=%async_computation.1 | async-start | bytes 786432 | tf_op jit(solution)/shard_map/all_to_all | solution.py:68
  13.4 0.7 convert_multiply_fusion
  14.1 2.2 %convolution_convert_fusion = bf16[768,512]{1,0:T(8,128)(2,1)} fusion(f32[256]{0:T(256)S(1)} %bitcast.73, f32[256]{0:T(256)S(1)} %bitcast.72, s32[256]{0:T(256)S(1)} %bitcast.70, s32[256]{0:T(256)S(1)} %bitcast.67, bf16[256,2048]{1,0:T(8,128)(2,1)} %param.7, s32[]{:T(128)S(6)} %select_n.66), kind=kOutput, calls=%fused_computation.22 | convolution fusion | flops 202506240 | bytes 1052676 | tf_op jit(solution)/shard_map/dot_general | solution.py:67
  16.3 8.8 %all-to-all-done.1 = bf16[8,96,256]{2,1,0:T(8,128)(2,1)S(1)} async-done(((bf16[8,96,256]{2,1,0:T(8,128)(2,1)}), bf16[8,96,256]{2,1,0:T(8,128)(2,1)S(1)}, u32[]{:S(2)}, u32[]{:S(2)}) %all-to-all-start.1) | async-done | bytes 393248 | tf_op jit(solution)/shard_map/all_to_all | solution.py:68
  25.1 3.6 %all-to-all-start = ((bf16[8,96,512]{2,1,0:T(8,128)(2,1)}), bf16[8,96,512]{2,1,0:T(8,128)(2,1)S(1)}, u32[]{:S(2)}, u32[]{:S(2)}) async-start(bf16[8,96,512]{2,1,0:T(8,128)(2,1)} %bitcast.63), calls=%async_computation | async-start | bytes 1572864 | tf_op jit(solution)/shard_map/all_to_all | solution.py:68
  28.8 1.5 %collective-permute-start.3 = (bf16[768,256]{1,0:T(8,128)(2,1)S(1)}, bf16[768,256]{1,0:T(8,128)(2,1)}, u32[]{:S(2)}, u32[]{:S(2)}) collective-permute-start(bf16[768,256]{1,0:T(8,128)(2,1)S(1)} %bitcast.60), channel_id=1, source_target_pairs={{0,2},{1,3},{2,0},{3,1},{4,6},{5,7},{6,4},{7,5},{8,10},{9,11},{10,... | collective-permute-start | bytes 1179656 | tf_op jit(solution)/shard_map/ppermute | solution.py:71
  30.3 18.6 %all-to-all-done = bf16[8,96,512]{2,1,0:T(8,128)(2,1)S(1)} async-done(((bf16[8,96,512]{2,1,0:T(8,128)(2,1)}), bf16[8,96,512]{2,1,0:T(8,128)(2,1)S(1)}, u32[]{:S(2)}, u32[]{:S(2)}) %all-to-all-start) | async-done | bytes 786464 | tf_op jit(solution)/shard_map/all_to_all | solution.py:68
  48.9 1.5 %collective-permute-start = (bf16[768,512]{1,0:T(8,128)(2,1)S(1)}, bf16[768,512]{1,0:T(8,128)(2,1)}, u32[]{:S(2)}, u32[]{:S(2)}) collective-permute-start(bf16[768,512]{1,0:T(8,128)(2,1)S(1)} %bitcast.57), channel_id=1, source_target_pairs={{0,2},{1,3},{2,0},{3,1},{4,6},{5,7},{6,4},{7,5},{8,10},{9,11},{10,... | collective-permute-start | bytes 2359304 | tf_op jit(solution)/shard_map/ppermute | solution.py:71
  50.4 0.5 collective-permute-start.5
  51.2 1.0 constant_dynamic-update-slice_fusion.2
  52.3 1.0 constant_dynamic-update-slice_fusion.1
  54.1 12.8 %collective-permute-done = bf16[768,512]{1,0:T(8,128)(2,1)} collective-permute-done((bf16[768,512]{1,0:T(8,128)(2,1)S(1)}, bf16[768,512]{1,0:T(8,128)(2,1)}, u32[]{:S(2)}, u32[]{:S(2)}) %collective-permute-start) | collective-permute-done | bytes 786464 | tf_op jit(solution)/shard_map/ppermute | solution.py:71
  66.9 3.5 %multiply_convert_fusion.2 = (bf16[768,1024]{1,0:T(8,128)(2,1)}, f32[768,1024]{1,0:T(8,128)S(1)}) fusion(bf16[768,1024]{1,0:T(8,128)(2,1)S(1)} %constant_dynamic-update-slice_fusion, bf16[1,1024,1024]{2,1,0:T(8,128)(2,1)S(1)} %copy-done), kind=kOutput, calls=%fused_computation.14 | convolution fusion | flops 1617690624 | bytes 8388608 | tf_op jit(solution)/shard_map/dot_general | solution.py:100
  70.4 1.4 %constant_dynamic-update-slice_fusion.6 = bf16[768,2048]{1,0:T(8,128)(2,1)S(1)} fusion(bf16[768,2048]{1,0:T(8,128)(2,1)S(1)} %constant_dynamic-update-slice_fusion.7, bf16[768,512]{1,0:T(8,128)(2,1)} %collective-permute-done, s32[]{:T(128)S(6)} %select_n.67), kind=kLoop, calls=%fused_computation.61 | loop fusion | bytes 1572868 | tf_op jit(solution)/shard_map/dynamic_update_slice | solution.py:82
  72.0 0.8 copy-done.2
  72.8 5.0 %fusion.9 = bf16[768,1024]{1,0:T(8,128)(2,1)S(1)} fusion(f32[768,1024]{1,0:T(8,128)S(1)} %get-tuple-element.12, bf16[768,2048]{1,0:T(8,128)(2,1)S(1)} %constant_dynamic-update-slice_fusion.4, bf16[1,1024,2048]{2,1,0:T(8,128)(2,1)S(1)} %copy-done.2), kind=kOutput, calls=%fused_computation.13 | convolution fusion | flops 3236954112 | bytes 12058624 | tf_op jit(solution)/shard_map/dot_general | solution.py:103
  77.8 1.8 %fusion.12 = f32[768,1024]{1,0:T(8,128)S(1)} fusion(bf16[768,1024]{1,0:T(8,128)(2,1)S(1)} %fusion.9, bf16[1,1024,1024]{2,1,0:T(8,128)(2,1)S(1)} %copy-done), kind=kOutput, calls=%fused_computation.15 | convolution fusion | flops 1610612736 | bytes 6815744 | tf_op jit(solution)/shard_map/dot_general | solution.py:107
  79.7 0.4 dynamic-slice_bitcast_fusion.3
  80.3 0.6 collective-permute-start.6
  80.9 3.0 %collective-permute-done.6 = f32[512,768]{0,1:T(8,128)S(1)} collective-permute-done((f32[512,768]{0,1:T(8,128)S(1)}, f32[512,768]{0,1:T(8,128)S(1)}, u32[]{:S(2)}, u32[]{:S(2)}) %collective-permute-start.6) | collective-permute-done | bytes 1572896 | tf_op jit(solution)/shard_map/ppermute | solution.py:34
  84.2 1.6 %collective-permute-start.7 = (bf16[256,768]{0,1:T(8,128)(2,1)S(1)}, bf16[256,768]{0,1:T(8,128)(2,1)S(1)}, u32[]{:S(2)}, u32[]{:S(2)}) collective-permute-start(bf16[256,768]{0,1:T(8,128)(2,1)S(1)} %slice.46), channel_id=1, source_target_pairs={{0,2},{1,3},{2,0},{3,1},{4,6},{5,7},{6,4},{7,5},{8,10},{9,11},{10,... | collective-permute-start | bytes 1179656 | tf_op jit(solution)/shard_map/ppermute | solution.py:36
  85.8 3.2 %fusion.16 = bf16[1,1024,1024]{2,1,0:T(8,128)(2,1)} fusion(bf16[768,1024]{1,0:T(8,128)(2,1)S(1)} %constant_dynamic-update-slice_fusion, bf16[768,1024]{1,0:T(8,128)(2,1)S(1)} %fusion.9), kind=kOutput, calls=%fused_computation.19 | convolution fusion | flops 1612709888 | bytes 5242880 | tf_op jit(solution)/shard_map/dot_general | solution.py:125
  89.0 6.7 %collective-permute-done.7 = bf16[256,768]{0,1:T(8,128)(2,1)S(1)} collective-permute-done((bf16[256,768]{0,1:T(8,128)(2,1)S(1)}, bf16[256,768]{0,1:T(8,128)(2,1)S(1)}, u32[]{:S(2)}, u32[]{:S(2)}) %collective-permute-start.7) | collective-permute-done | bytes 393248 | tf_op jit(solution)/shard_map/ppermute | solution.py:36
  95.7 0.9 fusion.17
  96.6 5.1 %all-to-all-start.2 = ((bf16[256,8,96]{0,2,1:T(8,128)(2,1)}), bf16[256,8,96]{0,2,1:T(8,128)(2,1)S(1)}, u32[]{:S(2)}, u32[]{:S(2)}) async-start(bf16[256,8,96]{0,2,1:T(8,128)(2,1)} %bitcast.20), calls=%async_computation.2 | async-start | bytes 786432 | tf_op jit(solution)/shard_map/all_to_all | solution.py:114
  101.7 7.9 %fusion.2 = bf16[1,1024,2048]{2,1,0:T(8,128)(2,1)} fusion(bf16[768,1024]{1,0:T(8,128)(2,1)} %get-tuple-element.11, bf16[768,2048]{1,0:T(8,128)(2,1)} %copy-done.1), kind=kOutput, calls=%fused_computation.6 | convolution fusion | flops 3225419776 | bytes 8912896 | tf_op jit(solution)/shard_map/dot_general | solution.py:128
  109.6 3.5 %all-to-all-done.2 = bf16[256,8,96]{0,2,1:T(8,128)(2,1)S(1)} async-done(((bf16[256,8,96]{0,2,1:T(8,128)(2,1)}), bf16[256,8,96]{0,2,1:T(8,128)(2,1)S(1)}, u32[]{:S(2)}, u32[]{:S(2)}) %all-to-all-start.2) | async-done | bytes 393248 | tf_op jit(solution)/shard_map/all_to_all | solution.py:114
  113.1 1.1 convolution_convert_fusion.2
  (33 shorter events, 2.5 us)
Async XLA Ops:
  0.6 66.2 %copy-start = (bf16[1,1024,1024]{2,1,0:T(8,128)(2,1)S(1)}, bf16[1,1024,1024]{2,1,0:T(8,128)(2,1)}, u32[]{:S(2)}) copy-start(bf16[1,1024,1024]{2,1,0:T(8,128)(2,1)} %param.10) | copy-start | bytes 6291460
  6.2 19.0 %all-to-all-start.1 = ((bf16[8,96,256]{2,1,0:T(8,128)(2,1)}), bf16[8,96,256]{2,1,0:T(8,128)(2,1)S(1)}, u32[]{:S(2)}, u32[]{:S(2)}) async-start(bf16[8,96,256]{2,1,0:T(8,128)(2,1)} %bitcast.13), calls=%async_computation.1 | async-start | bytes 786432 | tf_op jit(solution)/shard_map/all_to_all | solution.py:68
  25.1 23.8 %all-to-all-start = ((bf16[8,96,512]{2,1,0:T(8,128)(2,1)}), bf16[8,96,512]{2,1,0:T(8,128)(2,1)S(1)}, u32[]{:S(2)}, u32[]{:S(2)}) async-start(bf16[8,96,512]{2,1,0:T(8,128)(2,1)} %bitcast.63), calls=%async_computation | async-start | bytes 1572864 | tf_op jit(solution)/shard_map/all_to_all | solution.py:68
  28.8 21.7 %collective-permute-start.3 = (bf16[768,256]{1,0:T(8,128)(2,1)S(1)}, bf16[768,256]{1,0:T(8,128)(2,1)}, u32[]{:S(2)}, u32[]{:S(2)}) collective-permute-start(bf16[768,256]{1,0:T(8,128)(2,1)S(1)} %bitcast.60), channel_id=1, source_target_pairs={{0,2},{1,3},{2,0},{3,1},{4,6},{5,7},{6,4},{7,5},{8,10},{9,11},{10,... | collective-permute-start | bytes 1179656 | tf_op jit(solution)/shard_map/ppermute | solution.py:71
  48.9 18.0 %collective-permute-start = (bf16[768,512]{1,0:T(8,128)(2,1)S(1)}, bf16[768,512]{1,0:T(8,128)(2,1)}, u32[]{:S(2)}, u32[]{:S(2)}) collective-permute-start(bf16[768,512]{1,0:T(8,128)(2,1)S(1)} %bitcast.57), channel_id=1, source_target_pairs={{0,2},{1,3},{2,0},{3,1},{4,6},{5,7},{6,4},{7,5},{8,10},{9,11},{10,... | collective-permute-start | bytes 2359304 | tf_op jit(solution)/shard_map/ppermute | solution.py:71
  50.4 1.9 %collective-permute-start.4 = (bf16[768,256]{1,0:T(8,128)(2,1)S(1)}, bf16[768,256]{1,0:T(8,128)(2,1)}, u32[]{:S(2)}, u32[]{:S(2)}) collective-permute-start(bf16[768,256]{1,0:T(8,128)(2,1)S(1)} %bitcast.61), channel_id=1, source_target_pairs={{0,1},{1,0},{2,3},{3,2},{4,5},{5,4},{6,7},{7,6},{8,9},{9,8},{10,11... | collective-permute-start | bytes 1179656 | tf_op jit(solution)/shard_map/ppermute | solution.py:75
  50.4 3.6 %collective-permute-start.5 = (bf16[768,256]{1,0:T(8,128)(2,1)}, bf16[768,256]{1,0:T(8,128)(2,1)S(1)}, u32[]{:S(2)}, u32[]{:S(2)}) collective-permute-start(bf16[768,256]{1,0:T(8,128)(2,1)} %collective-permute-done.3), channel_id=1, source_target_pairs={{0,1},{1,0},{2,3},{3,2},{4,5},{5,4},{6,7},{7,6},{8,9},{9,8},{10,11... | collective-permute-start | bytes 1179656 | tf_op jit(solution)/shard_map/ppermute | solution.py:75
  53.3 18.5 %collective-permute-start.1 = (bf16[768,512]{1,0:T(8,128)(2,1)S(1)}, bf16[768,512]{1,0:T(8,128)(2,1)S(1)}, u32[]{:S(2)}, u32[]{:S(2)}) collective-permute-start(bf16[768,512]{1,0:T(8,128)(2,1)S(1)} %bitcast.58), channel_id=1, source_target_pairs={{0,1},{1,0},{2,3},{3,2},{4,5},{5,4},{6,7},{7,6},{8,9},{9,8},{10,11... | collective-permute-start | bytes 2359304 | tf_op jit(solution)/shard_map/ppermute | solution.py:75
  66.9 5.0 %collective-permute-start.2 = (bf16[768,512]{1,0:T(8,128)(2,1)}, bf16[768,512]{1,0:T(8,128)(2,1)S(1)}, u32[]{:S(2)}, u32[]{:S(2)}) collective-permute-start(bf16[768,512]{1,0:T(8,128)(2,1)} %collective-permute-done), channel_id=1, source_target_pairs={{0,1},{1,0},{2,3},{3,2},{4,5},{5,4},{6,7},{7,6},{8,9},{9,8},{10,11... | collective-permute-start | bytes 2359304 | tf_op jit(solution)/shard_map/ppermute | solution.py:75
  70.4 2.4 %copy-start.2 = (bf16[1,1024,2048]{2,1,0:T(8,128)(2,1)S(1)}, bf16[1,1024,2048]{2,1,0:T(8,128)(2,1)}, u32[]{:S(2)}) copy-start(bf16[1,1024,2048]{2,1,0:T(8,128)(2,1)} %param.11) | copy-start | bytes 12582916
  72.0 5.8 %copy-start.1 = (bf16[768,2048]{1,0:T(8,128)(2,1)}, bf16[768,2048]{1,0:T(8,128)(2,1)S(1)}, u32[]{:S(2)}) copy-start(bf16[768,2048]{1,0:T(8,128)(2,1)S(1)} %constant_dynamic-update-slice_fusion.4) | copy-start | bytes 9437188
  80.3 3.6 %collective-permute-start.6 = (f32[512,768]{0,1:T(8,128)S(1)}, f32[512,768]{0,1:T(8,128)S(1)}, u32[]{:S(2)}, u32[]{:S(2)}) collective-permute-start(f32[512,768]{0,1:T(8,128)S(1)} %pad_maximum_fusion), channel_id=1, source_target_pairs={{0,1},{1,0},{2,3},{3,2},{4,5},{5,4},{6,7},{7,6},{8,9},{9,8},{10,11... | collective-permute-start | bytes 4718600 | tf_op jit(solution)/shard_map/ppermute | solution.py:34
  84.2 11.5 %collective-permute-start.7 = (bf16[256,768]{0,1:T(8,128)(2,1)S(1)}, bf16[256,768]{0,1:T(8,128)(2,1)S(1)}, u32[]{:S(2)}, u32[]{:S(2)}) collective-permute-start(bf16[256,768]{0,1:T(8,128)(2,1)S(1)} %slice.46), channel_id=1, source_target_pairs={{0,2},{1,3},{2,0},{3,1},{4,6},{5,7},{6,4},{7,5},{8,10},{9,11},{10,... | collective-permute-start | bytes 1179656 | tf_op jit(solution)/shard_map/ppermute | solution.py:36
  96.6 16.5 %all-to-all-start.2 = ((bf16[256,8,96]{0,2,1:T(8,128)(2,1)}), bf16[256,8,96]{0,2,1:T(8,128)(2,1)S(1)}, u32[]{:S(2)}, u32[]{:S(2)}) async-start(bf16[256,8,96]{0,2,1:T(8,128)(2,1)} %bitcast.20), calls=%async_computation.2 | async-start | bytes 786432 | tf_op jit(solution)/shard_map/all_to_all | solution.py:114
where the time goes:
time: 115 us; the launch traced here: 114 us
  waiting for transfers between devices  53.5 us (47%)
  matrix products  26.6 us (23%)
  starting transfers between devices  22 us (19%)
  local copies, waits for them, and re-layouts  7.22 us (6%)
  other arithmetic  4.03 us (4%)
    all_to_all x2, waiting for transfers between devices, dispatched(): mine = lax.all_to_all(mine, 'ep', split_axis=0, concat_axis=0, tiled=True)  27.4 us
    ppermute x2, waiting for transfers between devices, dispatched(): across = lax.ppermute(mine, 'tp', [(i, i ^ 2) for i in range(tp_size)])  12.8 us
    all_to_all x2, starting transfers between devices, dispatched(): mine = lax.all_to_all(mine, 'ep', split_axis=0, concat_axis=0, tiled=True)  10.9 us
    dot_general x1, matrix products, span_grads(): lax.dot_general(act_cols, rows_dy, (((0,), (0,)), ((), ())), preferred_el...  7.86 us
    ppermute x1, waiting for transfers between devices, chip_then_link_sum(): lax.ppermute(send.astype(jnp.bfloat16), 'tp', [(i, i ^ 2) for i in range(...  6.71 us
    all_to_all x1, starting transfers between devices, shards(): lax.all_to_all(summed.astype(jnp.bfloat16), 'ep', split_axis=1, concat_ax...  5.11 us
    dot_general x1, matrix products, shards(): lax.dot_general(rows_dy, weight_out, (((1,), (1,)), ((), ())), preferred_...  5.04 us
    dot_general x2, matrix products, dispatched(): jnp.dot(selection, mine, preferred_element_type=jnp.float32)  4.14 us
  transfers between devices with their start and end apart: 11, of which 6 were waited for; matrix products, arithmetic and copies ran while one was open for 19% of the time, Pallas kernels for 0%

commit v1 on v0

--- a/solution.py
+++ b/solution.py
@@ -5,6 +5,27 @@
 from jax.sharding import PartitionSpec as P
 
 E = 8
+
+
+def refer_the_files(my_data, net_axis="ep"):
+    carry = jax.lax.psum(1, axis_name=net_axis)
+    r_now, v_next = (carry, jax.lax.axis_index(net_axis))
+    clean = my_data.shape[1] // r_now
+    current_block = list(my_data.shape)
+    current_block[1] = clean
+    tall = current_block[1]
+    current_block[1] = tall * r_now
+    seen_now = jnp.zeros(current_block, my_data.dtype)
+    c = 0
+    while c < r_now:
+        part_next = lax.dynamic_slice_in_dim(my_data, (v_next ^ c) * clean, clean, axis=1)
+        if c:
+            part_next = jax.lax.ppermute(
+                part_next, axis_name=net_axis, perm=[(no, no ^ c) for no in range(r_now)]
+            )
+        seen_now = lax.dynamic_update_slice_in_dim(seen_now, part_next, (v_next ^ c) * tall, axis=1)
+        c = c + 1
+    return seen_now
 
 
 def shifted(value, axis, by):
@@ -111,9 +132,7 @@
         summed = chip_then_link_sum(partial, tp_index)
     else:
         summed = lax.psum_scatter(partial, "tp", scatter_dimension=0, tiled=True)
-    returned = lax.all_to_all(
-        summed.astype(jnp.bfloat16), "ep", split_axis=1, concat_axis=1, tiled=True
-    )
+    returned = refer_the_files(summed.astype(jnp.bfloat16))
     grad_in = lax.dot_general(
         pick, returned, (((0,), (1,)), ((), ())), preferred_element_type=jnp.float32
     ).astype(jnp.bfloat16)

time: 115 us -> 124 us (1.078)
  starting transfers between devices: 22 us -> 26.5 us
  waiting for transfers between devices: 53.5 us -> 57.5 us
  matrix products: 26.6 us -> 23.8 us
  other arithmetic: 4.03 us -> 6.16 us
    ppermute x0 -> x7, starting transfers between devices: none -> 9.77 us  [refer_the_files(): jax.lax.ppermute(part_next, axis_name=net_axis, perm=[(no, no ^ c) for no...]
    ppermute x0 -> x7, waiting for transfers between devices: none -> 9.06 us  [refer_the_files(): jax.lax.ppermute(part_next, axis_name=net_axis, perm=[(no, no ^ c) for no...]
    all_to_all x1 -> x0, starting transfers between devices: 5.11 us -> none  [shards(): lax.all_to_all(summed.astype(jnp.bfloat16), 'ep', split_axis=1, concat_ax...]
    all_to_all x1 -> x0, waiting for transfers between devices: 3.54 us -> none  [shards(): lax.all_to_all(summed.astype(jnp.bfloat16), 'ep', split_axis=1, concat_ax...]
    dot_general x1, matrix products: 7.86 us -> 5.05 us  [span_grads(): lax.dot_general(act_cols, rows_dy, (((0,), (0,)), ((), ())), preferred_el...]
    ppermute x1, waiting for transfers between devices: 6.71 us -> 4.83 us  [chip_then_link_sum(): lax.ppermute(send.astype(jnp.bfloat16), 'tp', [(i, i ^ 2) for i in range(...]
    add x1, other arithmetic: 0.26 us -> 1.93 us  [chip_then_link_sum(): keep = keep + lax.ppermute(give, 'tp', [(i, i ^ 1) for i in range(4)])]
  transfers between devices with their start and end apart: 11 -> 17, of which waited for: 6 -> 7; matrix products, arithmetic and copies ran while one was open for 19% -> 15% of each run, Pallas kernels for 0% -> 0%
where the time goes in v1:
time: 124 us; the launch traced here: 123 us
  waiting for transfers between devices  57.5 us (46%)
  starting transfers between devices  26.5 us (21%)
  matrix products  23.8 us (19%)
  local copies, waits for them, and re-layouts  8.29 us (7%)
  other arithmetic  6.16 us (5%)
    all_to_all x2, waiting for transfers between devices, dispatched(): mine = lax.all_to_all(mine, 'ep', split_axis=0, concat_axis=0, tiled=True)  27.4 us
    ppermute x2, waiting for transfers between devices, dispatched(): across = lax.ppermute(mine, 'tp', [(i, i ^ 2) for i in range(tp_size)])  12.8 us
    all_to_all x2, starting transfers between devices, dispatched(): mine = lax.all_to_all(mine, 'ep', split_axis=0, concat_axis=0, tiled=True)  10.9 us
    ppermute x7, starting transfers between devices, refer_the_files(): jax.lax.ppermute(part_next, axis_name=net_axis, perm=[(no, no ^ c) for no...  9.77 us
    ppermute x7, waiting for transfers between devices, refer_the_files(): jax.lax.ppermute(part_next, axis_name=net_axis, perm=[(no, no ^ c) for no...  9.06 us
    dot_general x1, matrix products, span_grads(): lax.dot_general(act_cols, rows_dy, (((0,), (0,)), ((), ())), preferred_el...  5.05 us
    dot_general x1, matrix products, shards(): lax.dot_general(rows_dy, weight_out, (((1,), (1,)), ((), ())), preferred_...  5.05 us
    ppermute x1, waiting for transfers between devices, chip_then_link_sum(): lax.ppermute(send.astype(jnp.bfloat16), 'tp', [(i, i ^ 2) for i in range(...  4.83 us
  transfers between devices with their start and end apart: 17, of which 7 were waited for; matrix products, arithmetic and copies ran while one was open for 15% of the time, Pallas kernels for 0%

profile of v1, /device:TPU:0, one launch (start us, length us, event | category | flops | bytes accessed | tf_op | source)
XLA Modules:
  0.0 123.2 jit_solution(383504248467697663)
XLA Ops:
  0.7 1.0 copy.15
  1.8 1.1 reduce-window.6
  4.2 1.9 %convolution_convert_fusion.1 = bf16[768,256]{1,0:T(8,128)(2,1)} fusion(s32[256]{0:T(256)S(1)} %bitcast.66, s32[256]{0:T(256)S(1)} %bitcast.63, bf16[256,1024]{1,0:T(8,128)(2,1)} %param.6, s32[]{:T(128)S(6)} %select_n.102), kind=kOutput, calls=%fused_computation.23 | convolution fusion | flops 101449728 | bytes 526340 | tf_op jit(solution)/shard_map/dot_general | solution.py:88
  6.2 7.3 %all-to-all-start.1 = ((bf16[8,96,256]{2,1,0:T(8,128)(2,1)}), bf16[8,96,256]{2,1,0:T(8,128)(2,1)S(1)}, u32[]{:S(2)}, u32[]{:S(2)}) async-start(bf16[8,96,256]{2,1,0:T(8,128)(2,1)} %bitcast.13), calls=%async_computation.1 | async-start | bytes 786432 | tf_op jit(solution)/shard_map/all_to_all | solution.py:89
  14.1 2.2 %convolution_convert_fusion = bf16[768,512]{1,0:T(8,128)(2,1)} fusion(f32[256]{0:T(256)S(1)} %bitcast.70, f32[256]{0:T(256)S(1)} %bitcast.69, s32[256]{0:T(256)S(1)} %bitcast.67, s32[256]{0:T(256)S(1)} %bitcast.64, bf16[256,2048]{1,0:T(8,128)(2,1)} %param.7, s32[]{:T(128)S(6)} %select_n.98), kind=kOutput, calls=%fused_computation.22 | convolution fusion | flops 202506240 | bytes 1052676 | tf_op jit(solution)/shard_map/dot_general | solution.py:88
  16.3 8.8 %all-to-all-done.1 = bf16[8,96,256]{2,1,0:T(8,128)(2,1)S(1)} async-done(((bf16[8,96,256]{2,1,0:T(8,128)(2,1)}), bf16[8,96,256]{2,1,0:T(8,128)(2,1)S(1)}, u32[]{:S(2)}, u32[]{:S(2)}) %all-to-all-start.1) | async-done | bytes 393248 | tf_op jit(solution)/shard_map/all_to_all | solution.py:89
  25.1 3.6 %all-to-all-start = ((bf16[8,96,512]{2,1,0:T(8,128)(2,1)}), bf16[8,96,512]{2,1,0:T(8,128)(2,1)S(1)}, u32[]{:S(2)}, u32[]{:S(2)}) async-start(bf16[8,96,512]{2,1,0:T(8,128)(2,1)} %bitcast.61), calls=%async_computation | async-start | bytes 1572864 | tf_op jit(solution)/shard_map/all_to_all | solution.py:89
  28.8 1.5 %collective-permute-start.3 = (bf16[768,256]{1,0:T(8,128)(2,1)S(1)}, bf16[768,256]{1,0:T(8,128)(2,1)}, u32[]{:S(2)}, u32[]{:S(2)}) collective-permute-start(bf16[768,256]{1,0:T(8,128)(2,1)S(1)} %bitcast.58), channel_id=1, source_target_pairs={{0,2},{1,3},{2,0},{3,1},{4,6},{5,7},{6,4},{7,5},{8,10},{9,11},{10,... | collective-permute-start | bytes 1179656 | tf_op jit(solution)/shard_map/ppermute | solution.py:92
  30.3 18.6 %all-to-all-done = bf16[8,96,512]{2,1,0:T(8,128)(2,1)S(1)} async-done(((bf16[8,96,512]{2,1,0:T(8,128)(2,1)}), bf16[8,96,512]{2,1,0:T(8,128)(2,1)S(1)}, u32[]{:S(2)}, u32[]{:S(2)}) %all-to-all-start) | async-done | bytes 786464 | tf_op jit(solution)/shard_map/all_to_all | solution.py:89
  48.9 1.5 %collective-permute-start = (bf16[768,512]{1,0:T(8,128)(2,1)S(1)}, bf16[768,512]{1,0:T(8,128)(2,1)}, u32[]{:S(2)}, u32[]{:S(2)}) collective-permute-start(bf16[768,512]{1,0:T(8,128)(2,1)S(1)} %bitcast.55), channel_id=1, source_target_pairs={{0,2},{1,3},{2,0},{3,1},{4,6},{5,7},{6,4},{7,5},{8,10},{9,11},{10,... | collective-permute-start | bytes 2359304 | tf_op jit(solution)/shard_map/ppermute | solution.py:92
  51.2 1.0 constant_dynamic-update-slice_fusion.8
  52.3 1.0 constant_dynamic-update-slice_fusion.7
  54.1 12.8 %collective-permute-done = bf16[768,512]{1,0:T(8,128)(2,1)} collective-permute-done((bf16[768,512]{1,0:T(8,128)(2,1)S(1)}, bf16[768,512]{1,0:T(8,128)(2,1)}, u32[]{:S(2)}, u32[]{:S(2)}) %collective-permute-start) | collective-permute-done | bytes 786464 | tf_op jit(solution)/shard_map/ppermute | solution.py:92
  66.9 3.5 %multiply_convert_fusion.2 = (bf16[768,1024]{1,0:T(8,128)(2,1)}, f32[768,1024]{1,0:T(8,128)S(1)}) fusion(bf16[768,1024]{1,0:T(8,128)(2,1)S(1)} %constant_dynamic-update-slice_fusion.6, bf16[1,1024,1024]{2,1,0:T(8,128)(2,1)S(1)} %copy-done), kind=kOutput, calls=%fused_computation.14 | convolution fusion | flops 1617690624 | bytes 8388608 | tf_op jit(solution)/shard_map/dot_general | solution.py:121
  70.4 1.4 %constant_dynamic-update-slice_fusion.12 = bf16[768,2048]{1,0:T(8,128)(2,1)S(1)} fusion(bf16[768,2048]{1,0:T(8,128)(2,1)S(1)} %constant_dynamic-update-slice_fusion.13, bf16[768,512]{1,0:T(8,128)(2,1)} %collective-permute-done, s32[]{:T(128)S(6)} %select_n.99), kind=kLoop, calls=%fused_computation.75 | loop fusion | bytes 1572868 | tf_op jit(solution)/shard_map/dynamic_update_slice | solution.py:103
  72.8 5.0 %fusion.9 = bf16[768,1024]{1,0:T(8,128)(2,1)S(1)} fusion(f32[768,1024]{1,0:T(8,128)S(1)} %get-tuple-element.20, bf16[768,2048]{1,0:T(8,128)(2,1)S(1)} %constant_dynamic-update-slice_fusion.10, bf16[1,1024,2048]{2,1,0:T(8,128)(2,1)S(1)} %copy-done.5), kind=kOutput, calls=%fused_computation.13 | convolution fusion | flops 3236954112 | bytes 12058624 | tf_op jit(solution)/shard_map/dot_general | solution.py:124
  77.8 1.8 %fusion.12 = f32[768,1024]{1,0:T(8,128)S(1)} fusion(bf16[768,1024]{1,0:T(8,128)(2,1)S(1)} %fusion.9, bf16[1,1024,1024]{2,1,0:T(8,128)(2,1)S(1)} %copy-done), kind=kOutput, calls=%fused_computation.15 | convolution fusion | flops 1610612736 | bytes 6815744 | tf_op jit(solution)/shard_map/dot_general | solution.py:128
  79.7 1.3 %dynamic-slice_bitcast_fusion.3 = (f32[256,768]{0,1:T(8,128)S(1)}, f32[256,768]{0,1:T(8,128)S(1)}, f32[256,768]{0,1:T(8,128)S(1)}, f32[256,768]{0,1:T(8,128)}) fusion(f32[768,1024]{1,0:T(8,128)S(1)} %fusion.12, s32[]{:T(128)S(6)} %select_n.106, s32[]{:T(128)S(6)} %select_n.109, s32[]{:T(128)S(6)} %select_n.108, s32[]{:T(128)S(6)} %select_n.107), kind=kLoop, calls=%fused_computation.31 | loop fusion | bytes 6291472 | tf_op jit(solution)/shard_map/dynamic_slice | solution.py:51
  81.0 1.4 %pad_maximum_fusion = f32[512,768]{0,1:T(8,128)} fusion(f32[256,768]{0,1:T(8,128)S(1)} %get-tuple-element.4, f32[256,768]{0,1:T(8,128)S(1)} %get-tuple-element.5), kind=kLoop, calls=%fused_computation.21 | loop fusion | flops 393216 | bytes 3145728 | tf_op jit(solution)/shard_map/concatenate | solution.py:54
  82.9 3.4 %collective-permute-done.6 = f32[512,768]{0,1:T(8,128)} collective-permute-done((f32[512,768]{0,1:T(8,128)}, f32[512,768]{0,1:T(8,128)}, u32[]{:S(2)}, u32[]{:S(2)}) %collective-permute-start.6) | collective-permute-done | bytes 1572896 | tf_op jit(solution)/shard_map/ppermute | solution.py:55
  86.3 1.9 %maximum_add_fusion = f32[512,768]{0,1:T(8,128)S(1)} fusion(f32[512,768]{0,1:T(8,128)} %collective-permute-done.6, f32[256,768]{0,1:T(8,128)} %get-tuple-element.6, f32[256,768]{0,1:T(8,128)S(1)} %get-tuple-element.3), kind=kLoop, calls=%fused_computation.20 | loop fusion | flops 786432 | bytes 4718592 | tf_op jit(solution)/shard_map/add | solution.py:55
  88.3 1.6 %collective-permute-start.7 = (bf16[256,768]{0,1:T(8,128)(2,1)S(1)}, bf16[256,768]{0,1:T(8,128)(2,1)S(1)}, u32[]{:S(2)}, u32[]{:S(2)}) collective-permute-start(bf16[256,768]{0,1:T(8,128)(2,1)S(1)} %slice.46), channel_id=1, source_target_pairs={{0,2},{1,3},{2,0},{3,1},{4,6},{5,7},{6,4},{7,5},{8,10},{9,11},{10,... | collective-permute-start | bytes 1179656 | tf_op jit(solution)/shard_map/ppermute | solution.py:57
  89.9 5.0 %fusion.2 = bf16[1,1024,2048]{2,1,0:T(8,128)(2,1)} fusion(bf16[768,1024]{1,0:T(8,128)(2,1)S(1)} %copy-done.8, bf16[768,2048]{1,0:T(8,128)(2,1)S(1)} %copy-done.2), kind=kOutput, calls=%fused_computation.6 | convolution fusion | flops 3225419776 | bytes 8912896 | tf_op jit(solution)/shard_map/dot_general | solution.py:147
  94.9 4.8 %collective-permute-done.7 = bf16[256,768]{0,1:T(8,128)(2,1)S(1)} collective-permute-done((bf16[256,768]{0,1:T(8,128)(2,1)S(1)}, bf16[256,768]{0,1:T(8,128)(2,1)S(1)}, u32[]{:S(2)}, u32[]{:S(2)}) %collective-permute-start.7) | collective-permute-done | bytes 393248 | tf_op jit(solution)/shard_map/ppermute | solution.py:57
  100.0 2.1 %collective-permute-start.8 = (bf16[256,96]{0,1:T(8,128)(2,1)S(1)}, bf16[256,96]{0,1:T(8,128)(2,1)S(1)}, u32[]{:S(2)}, u32[]{:S(2)}) collective-permute-start(bf16[256,96]{0,1:T(8,128)(2,1)S(1)} %get-tuple-element.13), channel_id=1, source_target_pairs={{0,4},{4,0},{8,12},{12,8},{16,20},{20,16},{24,28},{28,24},{1,5},{5... | collective-permute-start | bytes 147464 | tf_op jit(solution)/shard_map/ppermute | solution.py:23
  102.1 3.2 %fusion.16 = bf16[1,1024,1024]{2,1,0:T(8,128)(2,1)} fusion(bf16[768,1024]{1,0:T(8,128)(2,1)S(1)} %copy-done.4, bf16[768,1024]{1,0:T(8,128)(2,1)S(1)} %copy-done.7), kind=kOutput, calls=%fused_computation.19 | convolution fusion | flops 1612709888 | bytes 5242880 | tf_op jit(solution)/shard_map/dot_general | solution.py:144
  105.3 1.8 %collective-permute-start.14 = (bf16[256,96]{0,1:T(8,128)(2,1)S(1)}, bf16[256,96]{0,1:T(8,128)(2,1)S(1)}, u32[]{:S(2)}, u32[]{:S(2)}) collective-permute-start(bf16[256,96]{0,1:T(8,128)(2,1)S(1)} %get-tuple-element.7), channel_id=1, source_target_pairs={{0,28},{4,24},{8,20},{12,16},{16,12},{20,8},{24,4},{28,0},{1,29},{... | collective-permute-start | bytes 147464 | tf_op jit(solution)/shard_map/ppermute | solution.py:23
  107.1 1.5 %collective-permute-start.13 = (bf16[256,96]{0,1:T(8,128)(2,1)S(1)}, bf16[256,96]{0,1:T(8,128)(2,1)S(1)}, u32[]{:S(2)}, u32[]{:S(2)}) collective-permute-start(bf16[256,96]{0,1:T(8,128)(2,1)S(1)} %get-tuple-element.8), channel_id=1, source_target_pairs={{0,24},{4,28},{8,16},{12,20},{16,8},{20,12},{24,0},{28,4},{1,25},{... | collective-permute-start | bytes 147464 | tf_op jit(solution)/shard_map/ppermute | solution.py:23
  108.6 4.4 %collective-permute-start.11 = (bf16[256,96]{0,1:T(8,128)(2,1)S(1)}, bf16[256,96]{0,1:T(8,128)(2,1)S(1)}, u32[]{:S(2)}, u32[]{:S(2)}) collective-permute-start(bf16[256,96]{0,1:T(8,128)(2,1)S(1)} %get-tuple-element.10), channel_id=1, source_target_pairs={{0,16},{4,20},{8,24},{12,28},{16,0},{20,4},{24,8},{28,12},{1,17},{... | collective-permute-start | bytes 147464 | tf_op jit(solution)/shard_map/ppermute | solution.py:23
  113.0 4.1 %collective-permute-done.9 = bf16[256,96]{0,1:T(8,128)(2,1)S(1)} collective-permute-done((bf16[256,96]{0,1:T(8,128)(2,1)S(1)}, bf16[256,96]{0,1:T(8,128)(2,1)S(1)}, u32[]{:S(2)}, u32[]{:S(2)}) %collective-permute-start.9) | collective-permute-done | bytes 49184 | tf_op jit(solution)/shard_map/ppermute | solution.py:23
  117.1 5.0 %collective-permute-done.10 = bf16[256,96]{0,1:T(8,128)(2,1)S(1)} collective-permute-done((bf16[256,96]{0,1:T(8,128)(2,1)S(1)}, bf16[256,96]{0,1:T(8,128)(2,1)S(1)}, u32[]{:S(2)}, u32[]{:S(2)}) %collective-permute-start.10) | collective-permute-done | bytes 49184 | tf_op jit(solution)/shard_map/ppermute | solution.py:23
  122.1 1.1 convolution_convert_fusion.2
  (66 shorter events, 5.5 us)
Async XLA Ops:
  0.6 66.2 %copy-start = (bf16[1,1024,1024]{2,1,0:T(8,128)(2,1)S(1)}, bf16[1,1024,1024]{2,1,0:T(8,128)(2,1)}, u32[]{:S(2)}) copy-start(bf16[1,1024,1024]{2,1,0:T(8,128)(2,1)} %param.10) | copy-start | bytes 6291460
  6.2 19.0 %all-to-all-start.1 = ((bf16[8,96,256]{2,1,0:T(8,128)(2,1)}), bf16[8,96,256]{2,1,0:T(8,128)(2,1)S(1)}, u32[]{:S(2)}, u32[]{:S(2)}) async-start(bf16[8,96,256]{2,1,0:T(8,128)(2,1)} %bitcast.13), calls=%async_computation.1 | async-start | bytes 786432 | tf_op jit(solution)/shard_map/all_to_all | solution.py:89
  25.1 23.8 %all-to-all-start = ((bf16[8,96,512]{2,1,0:T(8,128)(2,1)}), bf16[8,96,512]{2,1,0:T(8,128)(2,1)S(1)}, u32[]{:S(2)}, u32[]{:S(2)}) async-start(bf16[8,96,512]{2,1,0:T(8,128)(2,1)} %bitcast.61), calls=%async_computation | async-start | bytes 1572864 | tf_op jit(solution)/shard_map/all_to_all | solution.py:89
  28.8 21.7 %collective-permute-start.3 = (bf16[768,256]{1,0:T(8,128)(2,1)S(1)}, bf16[768,256]{1,0:T(8,128)(2,1)}, u32[]{:S(2)}, u32[]{:S(2)}) collective-permute-start(bf16[768,256]{1,0:T(8,128)(2,1)S(1)} %bitcast.58), channel_id=1, source_target_pairs={{0,2},{1,3},{2,0},{3,1},{4,6},{5,7},{6,4},{7,5},{8,10},{9,11},{10,... | collective-permute-start | bytes 1179656 | tf_op jit(solution)/shard_map/ppermute | solution.py:92
  48.9 18.0 %collective-permute-start = (bf16[768,512]{1,0:T(8,128)(2,1)S(1)}, bf16[768,512]{1,0:T(8,128)(2,1)}, u32[]{:S(2)}, u32[]{:S(2)}) collective-permute-start(bf16[768,512]{1,0:T(8,128)(2,1)S(1)} %bitcast.55), channel_id=1, source_target_pairs={{0,2},{1,3},{2,0},{3,1},{4,6},{5,7},{6,4},{7,5},{8,10},{9,11},{10,... | collective-permute-start | bytes 2359304 | tf_op jit(solution)/shard_map/ppermute | solution.py:92
  50.4 1.9 %collective-permute-start.4 = (bf16[768,256]{1,0:T(8,128)(2,1)S(1)}, bf16[768,256]{1,0:T(8,128)(2,1)}, u32[]{:S(2)}, u32[]{:S(2)}) collective-permute-start(bf16[768,256]{1,0:T(8,128)(2,1)S(1)} %bitcast.59), channel_id=1, source_target_pairs={{0,1},{1,0},{2,3},{3,2},{4,5},{5,4},{6,7},{7,6},{8,9},{9,8},{10,11... | collective-permute-start | bytes 1179656 | tf_op jit(solution)/shard_map/ppermute | solution.py:96
  50.4 3.6 %collective-permute-start.5 = (bf16[768,256]{1,0:T(8,128)(2,1)}, bf16[768,256]{1,0:T(8,128)(2,1)S(1)}, u32[]{:S(2)}, u32[]{:S(2)}) collective-permute-start(bf16[768,256]{1,0:T(8,128)(2,1)} %collective-permute-done.3), channel_id=1, source_target_pairs={{0,1},{1,0},{2,3},{3,2},{4,5},{5,4},{6,7},{7,6},{8,9},{9,8},{10,11... | collective-permute-start | bytes 1179656 | tf_op jit(solution)/shard_map/ppermute | solution.py:96
  53.3 18.5 %collective-permute-start.1 = (bf16[768,512]{1,0:T(8,128)(2,1)S(1)}, bf16[768,512]{1,0:T(8,128)(2,1)S(1)}, u32[]{:S(2)}, u32[]{:S(2)}) collective-permute-start(bf16[768,512]{1,0:T(8,128)(2,1)S(1)} %bitcast.56), channel_id=1, source_target_pairs={{0,1},{1,0},{2,3},{3,2},{4,5},{5,4},{6,7},{7,6},{8,9},{9,8},{10,11... | collective-permute-start | bytes 2359304 | tf_op jit(solution)/shard_map/ppermute | solution.py:96
  54.1 16.3 %copy-start.3 = (bf16[768,1024]{1,0:T(8,128)(2,1)}, bf16[768,1024]{1,0:T(8,128)(2,1)S(1)}, u32[]{:S(2)}) copy-start(bf16[768,1024]{1,0:T(8,128)(2,1)S(1)} %constant_dynamic-update-slice_fusion.6) | copy-start | bytes 4718596
  66.9 5.0 %collective-permute-start.2 = (bf16[768,512]{1,0:T(8,128)(2,1)}, bf16[768,512]{1,0:T(8,128)(2,1)S(1)}, u32[]{:S(2)}, u32[]{:S(2)}) collective-permute-start(bf16[768,512]{1,0:T(8,128)(2,1)} %collective-permute-done), channel_id=1, source_target_pairs={{0,1},{1,0},{2,3},{3,2},{4,5},{5,4},{6,7},{7,6},{8,9},{9,8},{10,11... | collective-permute-start | bytes 2359304 | tf_op jit(solution)/shard_map/ppermute | solution.py:96
  70.4 2.4 %copy-start.5 = (bf16[1,1024,2048]{2,1,0:T(8,128)(2,1)S(1)}, bf16[1,1024,2048]{2,1,0:T(8,128)(2,1)}, u32[]{:S(2)}) copy-start(bf16[1,1024,2048]{2,1,0:T(8,128)(2,1)} %param.11) | copy-start | bytes 12582916
  72.0 5.8 %copy-start.1 = (bf16[768,2048]{1,0:T(8,128)(2,1)}, bf16[768,2048]{1,0:T(8,128)(2,1)S(1)}, u32[]{:S(2)}) copy-start(bf16[768,2048]{1,0:T(8,128)(2,1)S(1)} %constant_dynamic-update-slice_fusion.10) | copy-start | bytes 9437188
  77.8 1.8 %copy-start.6 = (bf16[768,1024]{1,0:T(8,128)(2,1)}, bf16[768,1024]{1,0:T(8,128)(2,1)S(1)}, u32[]{:S(2)}) copy-start(bf16[768,1024]{1,0:T(8,128)(2,1)S(1)} %fusion.9) | copy-start | bytes 4718596
  82.4 3.9 %collective-permute-start.6 = (f32[512,768]{0,1:T(8,128)}, f32[512,768]{0,1:T(8,128)}, u32[]{:S(2)}, u32[]{:S(2)}) collective-permute-start(f32[512,768]{0,1:T(8,128)} %pad_maximum_fusion), channel_id=1, source_target_pairs={{0,1},{1,0},{2,3},{3,2},{4,5},{5,4},{6,7},{7,6},{8,9},{9,8},{10,11... | collective-permute-start | bytes 4718600 | tf_op jit(solution)/shard_map/ppermute | solution.py:55
  82.9 7.0 %copy-start.2 = (bf16[768,2048]{1,0:T(8,128)(2,1)S(1)}, bf16[768,2048]{1,0:T(8,128)(2,1)}, u32[]{:S(2)}) copy-start(bf16[768,2048]{1,0:T(8,128)(2,1)} %copy-done.1) | copy-start | bytes 9437188
  82.9 7.0 %copy-start.8 = (bf16[768,1024]{1,0:T(8,128)(2,1)S(1)}, bf16[768,1024]{1,0:T(8,128)(2,1)}, u32[]{:S(2)}) copy-start(bf16[768,1024]{1,0:T(8,128)(2,1)} %get-tuple-element.19) | copy-start | bytes 4718596
  88.3 13.8 %copy-start.4 = (bf16[768,1024]{1,0:T(8,128)(2,1)S(1)}, bf16[768,1024]{1,0:T(8,128)(2,1)}, u32[]{:S(2)}) copy-start(bf16[768,1024]{1,0:T(8,128)(2,1)} %copy-done.3) | copy-start | bytes 4718596
  88.3 13.8 %copy-start.7 = (bf16[768,1024]{1,0:T(8,128)(2,1)S(1)}, bf16[768,1024]{1,0:T(8,128)(2,1)}, u32[]{:S(2)}) copy-start(bf16[768,1024]{1,0:T(8,128)(2,1)} %copy-done.6) | copy-start | bytes 4718596
  88.3 11.5 %collective-permute-start.7 = (bf16[256,768]{0,1:T(8,128)(2,1)S(1)}, bf16[256,768]{0,1:T(8,128)(2,1)S(1)}, u32[]{:S(2)}, u32[]{:S(2)}) collective-permute-start(bf16[256,768]{0,1:T(8,128)(2,1)S(1)} %slice.46), channel_id=1, source_target_pairs={{0,2},{1,3},{2,0},{3,1},{4,6},{5,7},{6,4},{7,5},{8,10},{9,11},{10,... | collective-permute-start | bytes 1179656 | tf_op jit(solution)/shard_map/ppermute | solution.py:57
  100.0 12.9 %collective-permute-start.8 = (bf16[256,96]{0,1:T(8,128)(2,1)S(1)}, bf16[256,96]{0,1:T(8,128)(2,1)S(1)}, u32[]{:S(2)}, u32[]{:S(2)}) collective-permute-start(bf16[256,96]{0,1:T(8,128)(2,1)S(1)} %get-tuple-element.13), channel_id=1, source_target_pairs={{0,4},{4,0},{8,12},{12,8},{16,20},{20,16},{24,28},{28,24},{1,5},{5... | collective-permute-start | bytes 147464 | tf_op jit(solution)/shard_map/ppermute | solution.py:23
  105.3 16.8 %collective-permute-start.14 = (bf16[256,96]{0,1:T(8,128)(2,1)S(1)}, bf16[256,96]{0,1:T(8,128)(2,1)S(1)}, u32[]{:S(2)}, u32[]{:S(2)}) collective-permute-start(bf16[256,96]{0,1:T(8,128)(2,1)S(1)} %get-tuple-element.7), channel_id=1, source_target_pairs={{0,28},{4,24},{8,20},{12,16},{16,12},{20,8},{24,4},{28,0},{1,29},{... | collective-permute-start | bytes 147464 | tf_op jit(solution)/shard_map/ppermute | solution.py:23
  107.1 15.0 %collective-permute-start.13 = (bf16[256,96]{0,1:T(8,128)(2,1)S(1)}, bf16[256,96]{0,1:T(8,128)(2,1)S(1)}, u32[]{:S(2)}, u32[]{:S(2)}) collective-permute-start(bf16[256,96]{0,1:T(8,128)(2,1)S(1)} %get-tuple-element.8), channel_id=1, source_target_pairs={{0,24},{4,28},{8,16},{12,20},{16,8},{20,12},{24,0},{28,4},{1,25},{... | collective-permute-start | bytes 147464 | tf_op jit(solution)/shard_map/ppermute | solution.py:23
  108.6 13.5 %collective-permute-start.12 = (bf16[256,96]{0,1:T(8,128)(2,1)S(1)}, bf16[256,96]{0,1:T(8,128)(2,1)S(1)}, u32[]{:S(2)}, u32[]{:S(2)}) collective-permute-start(bf16[256,96]{0,1:T(8,128)(2,1)S(1)} %get-tuple-element.9), channel_id=1, source_target_pairs={{0,20},{4,16},{8,28},{12,24},{16,4},{20,0},{24,12},{28,8},{1,21},{... | collective-permute-start | bytes 147464 | tf_op jit(solution)/shard_map/ppermute | solution.py:23
  108.6 13.4 %collective-permute-start.11 = (bf16[256,96]{0,1:T(8,128)(2,1)S(1)}, bf16[256,96]{0,1:T(8,128)(2,1)S(1)}, u32[]{:S(2)}, u32[]{:S(2)}) collective-permute-start(bf16[256,96]{0,1:T(8,128)(2,1)S(1)} %get-tuple-element.10), channel_id=1, source_target_pairs={{0,16},{4,20},{8,24},{12,28},{16,0},{20,4},{24,8},{28,12},{1,17},{... | collective-permute-start | bytes 147464 | tf_op jit(solution)/shard_map/ppermute | solution.py:23
  112.9 4.1 %collective-permute-start.9 = (bf16[256,96]{0,1:T(8,128)(2,1)S(1)}, bf16[256,96]{0,1:T(8,128)(2,1)S(1)}, u32[]{:S(2)}, u32[]{:S(2)}) collective-permute-start(bf16[256,96]{0,1:T(8,128)(2,1)S(1)} %get-tuple-element.12), channel_id=1, source_target_pairs={{0,8},{4,12},{8,0},{12,4},{16,24},{20,28},{24,16},{28,20},{1,9},{5... | collective-permute-start | bytes 147464 | tf_op jit(solution)/shard_map/ppermute | solution.py:23
  117.0 5.0 %collective-permute-start.10 = (bf16[256,96]{0,1:T(8,128)(2,1)S(1)}, bf16[256,96]{0,1:T(8,128)(2,1)S(1)}, u32[]{:S(2)}, u32[]{:S(2)}) collective-permute-start(bf16[256,96]{0,1:T(8,128)(2,1)S(1)} %get-tuple-element.11), channel_id=1, source_target_pairs={{0,12},{4,8},{8,4},{12,0},{16,28},{20,24},{24,20},{28,16},{1,13},{... | collective-permute-start | bytes 147464 | tf_op jit(solution)/shard_map/ppermute | solution.py:23
